TPU v7x, 512 devices: a whole 4x8x8 slice. The times are simulated.
512 devices in a mesh: ctx: 64 (over x, y, core), fsdp: 8 (over z).
Axes of the slice: x: 4, y: 8, z: 8, core: 2. Of those that a mesh axis runs over, the one named last changes fastest.
Arguments:
- outer_gate: bfloat16 [2048, 16384], P('fsdp', 'ctx'), may hold values from -6 to 6
- inner_gate: bfloat16 [2048, 16384], P('fsdp', 'ctx'), may hold values from -6 to 6
- value_stream: bfloat16 [2048, 16384], P('fsdp', 'ctx'), may hold values from -6 to 6
- grad_output: bfloat16 [2048, 16384], P('fsdp', 'ctx'), may hold values from -6 to 6
- filters: float32 [128, 128], P('fsdp', 'ctx'), may hold values from -0.5 to 0.5
- feature_taps: float32 [3, 3, 2048], P(None, None, ('ctx', 'fsdp')), may hold values from -3 to 3
- skip_gain: float32 [2048], P(('ctx', 'fsdp')), may hold values from -4 to 4
Outputs:
- gated_out: bfloat16 [2048, 16384], P('fsdp', 'ctx')
- grad_outer: bfloat16 [2048, 16384], P('fsdp', 'ctx')
- grad_inner: bfloat16 [2048, 16384], P('fsdp', 'ctx')
- grad_value: bfloat16 [2048, 16384], P('fsdp', 'ctx')
- grad_filters: float32 [128, 128], P('fsdp', 'ctx')
- grad_taps: float32 [3, 3, 2048], P(None, None, ('ctx', 'fsdp'))
- grad_skip: float32 [2048], P(('ctx', 'fsdp'))
All inputs are finite; a program needn't handle non-finite values.
Results may differ from a plain program's by a relative error of at most 0.03.
Values may be sent and summed in bfloat16 or wider, within the bound.
No kernel may reach another device: no remote copies, remote signals or barrier semaphores. Data moves between devices by JAX's collectives and lax.ppermute only.
A program may use at most 64 MiB of HBM per device.

v0:
```python
import math
import jax
import jax.numpy as jnp
from jax import lax
from jax.sharding import PartitionSpec as P


def passed_along(shard, axis, by):
    devices = lax.axis_size(axis)
    pairs = [(i, i + by) for i in range(devices) if 0 <= i + by < devices]
    return lax.ppermute(shard, axis, pairs)


def featurize(extended, tap_gains):
    block_len = extended.shape[1] - 2
    result = tap_gains[0][:, None] * extended[:, 2:]
    result = result + tap_gains[1][:, None] * extended[:, 1 : block_len + 1]
    return result + tap_gains[2][:, None] * extended[:, :block_len]


def carry_back(extended, tap_gains):
    block_len = extended.shape[1] - 2
    result = tap_gains[0][:, None] * extended[:, :block_len]
    result = result + tap_gains[1][:, None] * extended[:, 1 : block_len + 1]
    return result + tap_gains[2][:, None] * extended[:, 2:]


def tap_sums(grad_rows, extended):
    block_len = grad_rows.shape[1]
    weighted = grad_rows.astype(jnp.float32)
    return jnp.stack(
        [
            jnp.sum(
                weighted * extended[:, 2 - shift_by : 2 - shift_by + block_len].astype(jnp.float32),
                axis=1,
            )
            for shift_by in range(3)
        ]
    )


def toeplitz_rows(filters_low, block_len):
    groups, taps_count = filters_low.shape
    window = block_len + taps_count - 1
    filter_row = jnp.concatenate(
        [filters_low[:, ::-1], jnp.zeros((groups, window + 1 - taps_count), filters_low.dtype)],
        axis=1,
    )
    flattened = jnp.tile(filter_row, (1, block_len))[:, : block_len * window]
    return flattened.reshape(groups, block_len, window)


def skew_sum(cross_terms, taps_count):
    groups, block_len, window = cross_terms.shape
    flattened = jnp.pad(cross_terms.reshape(groups, block_len * window), ((0, 0), (0, block_len)))
    return jnp.sum(flattened.reshape(groups, block_len, window + 1)[:, :, :taps_count], axis=1)[
        :, ::-1
    ]


def block_windows(extended, sub_len, reach_cols, groups):
    channels = extended.shape[0]
    block_len = extended.shape[1] - reach_cols
    count = block_len // sub_len
    lead = extended[:, :block_len].reshape(channels, count, sub_len)[:, :, :reach_cols]
    main = extended[:, reach_cols:].reshape(channels, count, sub_len)
    joined = jnp.concatenate([lead, main], axis=2)
    return joined.reshape(groups, channels // groups, count, sub_len + reach_cols)


def shards(outer_gate, inner_gate, value_stream, grad_output, filters, feature_taps, skip_gain):
    filters_all = lax.all_gather(filters, "ctx", axis=1, tiled=True)
    taps_every, skip_every = (
        lax.all_gather(feature_taps, ("ctx", "fsdp"), axis=2, tiled=True),
        lax.all_gather(skip_gain, ("ctx", "fsdp"), axis=0, tiled=True),
    )
    channels, block_len = outer_gate.shape
    chan_start = lax.axis_index("fsdp") * channels
    taps_all = lax.dynamic_slice_in_dim(taps_every, chan_start, channels, 2)
    skip_all = lax.dynamic_slice_in_dim(skip_every, chan_start, channels, 0)
    groups, taps_count = filters_all.shape
    group_size = channels // groups
    reach_cols = taps_count - 1
    count = block_len // block_len
    window = block_len + reach_cols
    feature_rims = passed_along(
        (
            outer_gate[:, block_len - 2 :],
            inner_gate[:, block_len - 2 :],
            value_stream[:, block_len - 2 :],
        ),
        "ctx",
        1,
    )
    outer_ext = jnp.concatenate([feature_rims[0], outer_gate], axis=1)
    inner_ext = jnp.concatenate([feature_rims[1], inner_gate], axis=1)
    value_ext = jnp.concatenate([feature_rims[2], value_stream], axis=1)
    outer_feat = featurize(outer_ext.astype(jnp.float32), taps_all[0])
    inner_feat = featurize(inner_ext.astype(jnp.float32), taps_all[1])
    value_feat = featurize(value_ext.astype(jnp.float32), taps_all[2])
    product = (inner_feat * value_feat).astype(jnp.bfloat16)
    product_rim = passed_along(product[:, block_len - reach_cols :], "ctx", 1)
    product_ext = jnp.concatenate([product_rim, product], axis=1)
    toeplitz = toeplitz_rows(filters_all.astype(jnp.bfloat16), block_len)
    windows = block_windows(product_ext, block_len, reach_cols, groups)
    convolved = jnp.einsum(
        "gcns,gts->gcnt", windows, toeplitz, preferred_element_type=jnp.float32
    ).reshape(channels, block_len)
    mixed = convolved + skip_all[:, None] * product.astype(jnp.float32)
    gated_out = (outer_feat * mixed).astype(jnp.bfloat16)
    upstream = grad_output.astype(jnp.float32)
    grad_mixed = (upstream * outer_feat).astype(jnp.bfloat16)
    grad_outer_feat = (upstream * mixed).astype(jnp.bfloat16)
    grad_groups = grad_mixed.reshape(groups, group_size, count, block_len)
    direct_term = skip_all[:, None] * grad_mixed.astype(jnp.float32)
    ahead_rims = passed_along((grad_mixed[:, :reach_cols], grad_outer_feat[:, :2]), "ctx", -1)
    mixed_ext = jnp.concatenate([grad_mixed, ahead_rims[0]], axis=1)
    flipped = block_windows(mixed_ext[:, ::-1], block_len, reach_cols, groups)
    reversed_out = jnp.einsum(
        "gcns,gts->gcnt", flipped, toeplitz, preferred_element_type=jnp.float32
    ).reshape(channels, block_len)
    grad_product = reversed_out[:, ::-1] + direct_term
    grad_inner_feat = (grad_product * value_feat).astype(jnp.bfloat16)
    grad_value_feat = (grad_product * inner_feat).astype(jnp.bfloat16)
    later_rims = passed_along((grad_inner_feat[:, :2], grad_value_feat[:, :2]), "ctx", -1)
    grad_outer = carry_back(
        jnp.concatenate([grad_outer_feat, ahead_rims[1]], axis=1).astype(jnp.float32), taps_all[0]
    )
    grad_inner = carry_back(
        jnp.concatenate([grad_inner_feat, later_rims[0]], axis=1).astype(jnp.float32), taps_all[1]
    )
    grad_value = carry_back(
        jnp.concatenate([grad_value_feat, later_rims[1]], axis=1).astype(jnp.float32), taps_all[2]
    )
    grad_scale = 1.0 / math.sqrt(lax.axis_size("ctx") * block_len)
    group_block = math.gcd(groups, 4)

    def cross_block(block_pair):
        grad_part, window_part = block_pair
        cross_terms = jnp.einsum(
            "gcnt,gcns->gts", grad_part, window_part, preferred_element_type=jnp.float32
        )
        return skew_sum(cross_terms, taps_count)

    filter_part = lax.map(
        cross_block,
        (
            grad_groups.reshape(groups // group_block, group_block, group_size, count, block_len),
            windows.reshape(groups // group_block, group_block, group_size, count, window),
        ),
    )
    filter_part = grad_scale * filter_part.reshape(groups, taps_count)
    skip_part = grad_scale * jnp.sum(
        grad_mixed.astype(jnp.float32) * product.astype(jnp.float32), axis=1
    )
    taps_part = grad_scale * jnp.stack(
        [
            tap_sums(grad_outer_feat, outer_ext),
            tap_sums(grad_inner_feat, inner_ext),
            tap_sums(grad_value_feat, value_ext),
        ]
    )
    filter_share = lax.psum_scatter(filter_part, "ctx", scatter_dimension=1, tiled=True)
    whole_taps = lax.dynamic_update_slice_in_dim(
        jnp.zeros(taps_every.shape, jnp.float32), taps_part, chan_start, 2
    )
    whole_skip = lax.dynamic_update_slice_in_dim(
        jnp.zeros(skip_every.shape, jnp.float32), skip_part, chan_start, 0
    )
    taps_share, skip_share = (
        lax.psum_scatter(whole_taps, ("ctx", "fsdp"), scatter_dimension=2, tiled=True),
        lax.psum_scatter(whole_skip, ("ctx", "fsdp"), scatter_dimension=0, tiled=True),
    )
    return (
        gated_out,
        grad_outer.astype(jnp.bfloat16),
        grad_inner.astype(jnp.bfloat16),
        grad_value.astype(jnp.bfloat16),
        filter_share,
        taps_share,
        skip_share,
    )


def solution(mesh):
    return jax.shard_map(
        shards,
        mesh=mesh,
        in_specs=(
            P("fsdp", "ctx"),
            P("fsdp", "ctx"),
            P("fsdp", "ctx"),
            P("fsdp", "ctx"),
            P("fsdp", "ctx"),
            P(None, None, ("ctx", "fsdp")),
            P(("ctx", "fsdp")),
        ),
        out_specs=(
            P("fsdp", "ctx"),
            P("fsdp", "ctx"),
            P("fsdp", "ctx"),
            P("fsdp", "ctx"),
            P("fsdp", "ctx"),
            P(None, None, ("ctx", "fsdp")),
            P(("ctx", "fsdp")),
        ),
        check_vma=False,
    )
```

profile of v0, /device:TPU:1, one launch (start us, length us, event | category | flops | bytes accessed | tf_op | source)
XLA Modules:
  0.0 771.6 jit_solution(13353346881446021520)
XLA Ops:
  7.2 1.6 slice.185
  8.8 4.6 collective-permute-start
  13.4 1.6 slice.199
  14.9 1.9 collective-permute-start.2
  16.9 1.6 slice.192
  18.4 3.6 collective-permute-start.1
  22.8 142.3 %all_gather.9 = f32[3,3,2048]{1,0,2:T(4,128)} all-gather(f32[3,3,4]{1,0,2:T(4,128)S(1)} %copy.30), channel_id=1, replica_groups=mesh['ctx'=64,'fsdp'=8] {'ctx','fsdp'}, dimensions={2}, use_global_device_ids=true | all-gather | bytes 73872 | tf_op jit(solution)/shard_map/all_gather | solution.py:74
  165.2 35.0 %all-gather = bf16[64,2,16]{2,1,0:T(2,128)(2,1)S(1)} all-gather(bf16[1,2,16]{2,1,0:T(2,128)(2,1)S(1)} %bitcast_convert_fusion), channel_id=1, replica_groups=mesh['ctx'=64,'fsdp'=8] {'ctx'}, dimensions={0}, use_global_device_ids=true | all-gather | bytes 4160 | tf_op jit(solution)/shard_map/all_gather | solution.py:72
  200.5 1.9 copy.41
  202.4 11.8 %dynamic-slice_reduce_fusion.2 = (f32[256]{0:T(256)S(1)}, f32[256]{0:T(256)S(1)}, f32[256]{0:T(256)}, f32[256]{0:T(256)}, f32[256]{0:T(256)}, /*index=5*/f32[256]{0:T(256)}, f32[256]{0:T(256)}, f32[256]{0:T(256)}, f32[256]{0:T(256)}) fusion(f32[3,3,2048]{1,0,2:T(4,128)} %all_gather.9, s32[]{:T(128)S(6)} %add.97, s32[]{:T(128)S(6)} %select_n.2, s32[]{:T(128)S(6)} %add.96), kind=kLoop, calls=%fused_computation.115 | loop fusion | bytes 18444 | tf_op jit(solution)/shard_map/slice | solution.py:16
  214.2 1.9 slice.244
  216.1 9.4 %reshape.115 = bf16[16,256,383]{2,1,0:T(8,128)(2,1)S(1)} reshape(bf16[16,98048]{1,0:T(8,128)(2,1)} %slice.244) | data formatting | bytes 6275072 | tf_op jit(solution)/shard_map/reshape | solution.py:50
  231.2 2.6 fusion.10
  234.6 2.9 collective-permute-start.3
  239.8 95.0 %all-reduce.6 = (f32[2048]{0:T(1024)}, f32[2048]{0:T(1024)}) all-reduce(f32[2048]{0:T(1024)S(1)} %dynamic-update-slice, f32[2048]{0:T(1024)S(1)} %multiply_dynamic-update-slice_fusion), channel_id=1, replica_groups=mesh['ctx'=64,'fsdp'=8] {'ctx','fsdp'}, use_global_device_ids=true, to_apply=%add.2 | all-reduce | flops 4096 | bytes 32768
  335.6 2.6 collective-permute-start.5
  341.3 2.5 fusion.12
  345.1 1.9 collective-permute-start.4
  349.5 2.5 fusion.41
  352.1 1.9 rev.14
  354.0 2.6 fusion.18
  357.3 1.9 collective-permute-start.6
  359.8 1.9 collective-permute-start.7
  361.8 1.6 pad_maximum_fusion.3
  363.4 15.8 %while.12 = (s32[]{:T(128)}, f32[4,4,128]{2,1,0:T(4,128)}, bf16[4,4,16,1,256]{4,2,1,3,0:T(8,128)(2,1)S(1)}, bf16[4,4,16,1,383]{4,2,1,3,0:T(8,128)(2,1)}, s32[]{:T(128)}, /*index=5*/f32[]{:T(128)}) while((s32[]{:T(128)}, f32[4,4,128]{2,1,0:T(4,128)}, bf16[4,4,16,1,256]{4,2,1,3,0:T(8,128)(2,1)S(1)}, bf16[4,4,16,1,383]{4,2,1,3,0:T(8,128)(2,1)}, ...), condition=%wide.region_2.3_spmd, body=%wide.region_0.2_spmd.sunk | while | flops 12680706 | bytes 11611221 | solution.py:145
  364.7 1.6 reshape.140
  368.6 1.6 reshape.140
  372.6 1.6 reshape.140
  376.5 1.6 reshape.140
  380.0 126.0 %all-reduce.3 = f32[16,128]{1,0:T(8,128)S(1)} all-reduce(f32[16,128]{1,0:T(8,128)S(1)} %bitcast.98), channel_id=2, replica_groups=mesh['ctx'=64,'fsdp'=8] {'ctx'}, use_global_device_ids=true, to_apply=%region_3.4.clone | all-reduce | flops 2048 | bytes 16384
  509.1 1.6 fusion.27
  514.6 248.8 %all-reduce.9.cloned.1.call-done = f32[3,3,2048]{2,1,0:T(4,128)} async-done(((f32[3,3,2048]{2,1,0:T(4,128)}), f32[3,3,2048]{2,1,0:T(4,128)}) %all-reduce.9.cloned.1.call-update) | async-done | bytes 73744
  (116 shorter events, 36.5 us)
Async XLA Ops:
  7.2 158.0 %copy-start.19 = (f32[16,2]{0,1:T(2,128)S(1)}, f32[16,2]{0,1:T(2,128)}, u32[]{:S(2)}) copy-start(f32[16,2]{0,1:T(2,128)} %param.13) | copy-start | bytes 388
  7.2 756.2 %all-reduce.9.cloned.1.call-start = ((), (), s32[]{:S(2)}) async-start(), calls=%async_computation | async-start | bytes 196608
  8.8 221.4 %collective-permute-start = (bf16[256,2]{1,0:T(8,128)(2,1)}, bf16[256,2]{1,0:T(8,128)(2,1)}, u32[]{:S(2)}, u32[]{:S(2)}) collective-permute-start(bf16[256,2]{1,0:T(8,128)(2,1)} %slice.185), channel_id=1, source_target_pairs={{0,8},{8,16},{16,24},{24,32},{32,40},{40,48},{48,56},{56,64},{64,7... | collective-permute-start | bytes 3080 | tf_op jit(solution)/shard_map/ppermute | solution.py:11
  14.9 213.3 %collective-permute-start.2 = (bf16[256,2]{1,0:T(8,128)(2,1)}, bf16[256,2]{1,0:T(8,128)(2,1)}, u32[]{:S(2)}, u32[]{:S(2)}) collective-permute-start(bf16[256,2]{1,0:T(8,128)(2,1)} %slice.199), channel_id=1, source_target_pairs={{0,8},{8,16},{16,24},{24,32},{32,40},{40,48},{48,56},{56,64},{64,7... | collective-permute-start | bytes 3080 | tf_op jit(solution)/shard_map/ppermute | solution.py:11
  18.4 210.8 %collective-permute-start.1 = (bf16[256,2]{1,0:T(8,128)(2,1)}, bf16[256,2]{1,0:T(8,128)(2,1)}, u32[]{:S(2)}, u32[]{:S(2)}) collective-permute-start(bf16[256,2]{1,0:T(8,128)(2,1)} %slice.192), channel_id=1, source_target_pairs={{0,8},{8,16},{16,24},{24,32},{32,40},{40,48},{48,56},{56,64},{64,7... | collective-permute-start | bytes 3080 | tf_op jit(solution)/shard_map/ppermute | solution.py:11
  214.2 17.0 %copy-start.10 = (f32[256]{0:T(256)}, f32[256]{0:T(256)S(1)}, u32[]{:S(2)}) copy-start(f32[256]{0:T(256)S(1)} %get-tuple-element.98) | copy-start | bytes 3076
  214.2 17.0 %copy-start.12 = (f32[256]{0:T(256)}, f32[256]{0:T(256)S(1)}, u32[]{:S(2)}) copy-start(f32[256]{0:T(256)S(1)} %get-tuple-element.99) | copy-start | bytes 3076
  216.1 12.2 %copy-start.4 = (bf16[256,256]{1,0:T(8,128)(2,1)S(1)}, bf16[256,256]{1,0:T(8,128)(2,1)}, u32[]{:S(2)}) copy-start(bf16[256,256]{1,0:T(8,128)(2,1)} %param.11) | copy-start | bytes 393220
  216.1 13.2 %copy-start.5 = (bf16[256,256]{1,0:T(8,128)(2,1)S(1)}, bf16[256,256]{1,0:T(8,128)(2,1)}, u32[]{:S(2)}) copy-start(bf16[256,256]{1,0:T(8,128)(2,1)} %param.10) | copy-start | bytes 393220
  216.1 14.2 %copy-start.1 = (bf16[256,256]{1,0:T(8,128)(2,1)S(1)}, bf16[256,256]{1,0:T(8,128)(2,1)}, u32[]{:S(2)}) copy-start(bf16[256,256]{1,0:T(8,128)(2,1)} %param.9) | copy-start | bytes 393220
  234.6 104.9 %collective-permute-start.3 = (bf16[256,127]{1,0:T(8,128)(2,1)}, bf16[256,127]{1,0:T(8,128)(2,1)}, u32[]{:S(2)}, u32[]{:S(2)}) collective-permute-start(bf16[256,127]{1,0:T(8,128)(2,1)} %slice.242), channel_id=1, source_target_pairs={{0,8},{8,16},{16,24},{24,32},{32,40},{40,48},{48,56},{56,64},{64,7... | collective-permute-start | bytes 195080 | tf_op jit(solution)/shard_map/ppermute | solution.py:11
  334.8 6.5 copy-start
  334.8 6.5 copy-start.8
  335.6 11.4 %collective-permute-start.5 = (bf16[256,127]{1,0:T(8,128)(2,1)}, bf16[256,127]{1,0:T(8,128)(2,1)S(1)}, u32[]{:S(2)}, u32[]{:S(2)}) collective-permute-start(bf16[256,127]{1,0:T(8,128)(2,1)} %slice.249), channel_id=1, source_target_pairs={{8,0},{16,8},{24,16},{32,24},{40,32},{48,40},{56,48},{64,56},{72,6... | collective-permute-start | bytes 195080 | tf_op jit(solution)/shard_map/ppermute | solution.py:11
  340.4 4.7 copy-start.7
  343.8 0.7 copy-start.2
  345.1 163.1 %collective-permute-start.4 = (bf16[256,2]{1,0:T(8,128)(2,1)}, bf16[256,2]{1,0:T(8,128)(2,1)}, u32[]{:S(2)}, u32[]{:S(2)}) collective-permute-start(bf16[256,2]{1,0:T(8,128)(2,1)} %slice.245), channel_id=1, source_target_pairs={{8,0},{16,8},{24,16},{32,24},{40,32},{48,40},{56,48},{64,56},{72,6... | collective-permute-start | bytes 3080 | tf_op jit(solution)/shard_map/ppermute | solution.py:11
  356.6 6.8 copy-start.6
  357.3 153.4 %collective-permute-start.6 = (bf16[256,2]{1,0:T(8,128)(2,1)}, bf16[256,2]{1,0:T(8,128)(2,1)}, u32[]{:S(2)}, u32[]{:S(2)}) collective-permute-start(bf16[256,2]{1,0:T(8,128)(2,1)} %slice.251), channel_id=1, source_target_pairs={{8,0},{16,8},{24,16},{32,24},{40,32},{48,40},{56,48},{64,56},{72,6... | collective-permute-start | bytes 3080 | tf_op jit(solution)/shard_map/ppermute | solution.py:11
  359.8 152.9 %collective-permute-start.7 = (bf16[256,2]{1,0:T(8,128)(2,1)}, bf16[256,2]{1,0:T(8,128)(2,1)}, u32[]{:S(2)}, u32[]{:S(2)}) collective-permute-start(bf16[256,2]{1,0:T(8,128)(2,1)} %slice.255), channel_id=1, source_target_pairs={{8,0},{16,8},{24,16},{32,24},{40,32},{48,40},{56,48},{64,56},{72,6... | collective-permute-start | bytes 3080 | tf_op jit(solution)/shard_map/ppermute | solution.py:11
  363.4 144.8 %copy-start.3 = (bf16[256,256]{1,0:T(8,128)(2,1)S(1)}, bf16[256,256]{1,0:T(8,128)(2,1)}, u32[]{:S(2)}) copy-start(bf16[256,256]{1,0:T(8,128)(2,1)} %copy-done.2) | copy-start | bytes 393220
  363.4 145.7 %copy-start.18 = (f32[256]{0:T(256)S(1)}, f32[256]{0:T(256)}, u32[]{:S(2)}) copy-start(f32[256]{0:T(256)} %get-tuple-element.103) | copy-start | bytes 3076
  363.4 148.3 %copy-start.15 = (f32[256]{0:T(256)S(1)}, f32[256]{0:T(256)}, u32[]{:S(2)}) copy-start(f32[256]{0:T(256)} %get-tuple-element.100) | copy-start | bytes 3076
  363.4 148.3 %copy-start.16 = (f32[256]{0:T(256)S(1)}, f32[256]{0:T(256)}, u32[]{:S(2)}) copy-start(f32[256]{0:T(256)} %get-tuple-element.101) | copy-start | bytes 3076
  363.4 148.3 %copy-start.17 = (f32[256]{0:T(256)S(1)}, f32[256]{0:T(256)}, u32[]{:S(2)}) copy-start(f32[256]{0:T(256)} %get-tuple-element.102) | copy-start | bytes 3076
  379.3 134.3 %copy-start.11 = (f32[256]{0:T(256)S(1)}, f32[256]{0:T(256)}, u32[]{:S(2)}) copy-start(f32[256]{0:T(256)} %copy-done.10) | copy-start | bytes 3076
  379.3 134.3 %copy-start.13 = (f32[256]{0:T(256)S(1)}, f32[256]{0:T(256)}, u32[]{:S(2)}) copy-start(f32[256]{0:T(256)} %copy-done.12) | copy-start | bytes 3076
  379.3 134.4 %copy-start.14 = (f32[256]{0:T(256)S(1)}, f32[256]{0:T(256)}, u32[]{:S(2)}) copy-start(f32[256]{0:T(256)} %get-tuple-element.106) | copy-start | bytes 3076
  507.4 0.7 copy-start.9
Sparse Core Ops, SparseCore 0:
  508.3 255.0 all-reduce.8
where the time goes:
time: 773 us; the launch traced here: 772 us
  blocking collectives  398 us (51%)
  waiting for transfers between devices  249 us (32%)
  local copies, waits for them, and re-layouts  57.5 us (7%)
  other arithmetic  22.1 us (3%)
  starting transfers between devices  21.3 us (3%)
  between operations  15.1 us (2%)
  matrix products  8.32 us (1%)
    unnamed x2, waiting for transfers between devices  249 us
    unnamed x2, blocking collectives  221 us
    all_gather x1, blocking collectives, shards(): lax.all_gather(feature_taps, ('ctx', 'fsdp'), axis=2, tiled=True)  142 us
    all_gather x1, blocking collectives, shards(): filters_all = lax.all_gather(filters, 'ctx', axis=1, tiled=True)  35 us
    ppermute x8, starting transfers between devices, passed_along(): return lax.ppermute(shard, axis, pairs)  21.3 us
  transfers between devices with their start and end apart: 9, of which 1 were waited for; matrix products, arithmetic and copies ran while one was open for 10% of the time, Pallas kernels for 0%

commit v1 on v0

--- a/solution.py
+++ b/solution.py
@@ -71,7 +71,12 @@
 def shards(outer_gate, inner_gate, value_stream, grad_output, filters, feature_taps, skip_gain):
     filters_all = lax.all_gather(filters, "ctx", axis=1, tiled=True)
     taps_every, skip_every = (
-        lax.all_gather(feature_taps, ("ctx", "fsdp"), axis=2, tiled=True),
+        jnp.concatenate(
+            lax.all_to_all(
+                jnp.stack([feature_taps] * lax.axis_size(("ctx", "fsdp"))), ("ctx", "fsdp"), 0, 0
+            ),
+            axis=2,
+        ),
         lax.all_gather(skip_gain, ("ctx", "fsdp"), axis=0, tiled=True),
     )
     channels, block_len = outer_gate.shape

time: 773 us -> 714 us (0.924)
  blocking collectives: 398 us -> 317 us
  starting transfers between devices: 21.3 us -> 42.6 us
    all_gather x1 -> x0, blocking collectives: 142 us -> none  [shards(): lax.all_gather(feature_taps, ('ctx', 'fsdp'), axis=2, tiled=True)]
    all_gather x1, blocking collectives: 35 us -> 90.5 us  [shards(): filters_all = lax.all_gather(filters, 'ctx', axis=1, tiled=True)]
    all_to_all x0 -> x1, starting transfers between devices: none -> 22.1 us  [shards(): lax.all_to_all(jnp.stack([feature_taps] * lax.axis_size(('ctx', 'fsdp')))...]
    slice x1, local copies, waits for them, and re-layouts: 11.8 us -> 0.09 us  [featurize(): result = tap_gains[0][:, None] * extended[:, 2:]]
  transfers between devices with their start and end apart: 9 -> 10, of which waited for: 1 -> 1; matrix products, arithmetic and copies ran while one was open for 10% -> 10% of each run, Pallas kernels for 0% -> 0%
where the time goes in v1:
time: 714 us; the launch traced here: 712 us
  blocking collectives  317 us (44%)
  waiting for transfers between devices  251 us (35%)
  local copies, waits for them, and re-layouts  56.5 us (8%)
  starting transfers between devices  42.6 us (6%)
  other arithmetic  24.8 us (3%)
  between operations  15.2 us (2%)
    unnamed x2, waiting for transfers between devices  251 us
    unnamed x2, blocking collectives  226 us
    all_gather x1, blocking collectives, shards(): filters_all = lax.all_gather(filters, 'ctx', axis=1, tiled=True)  90.5 us
    all_to_all x1, starting transfers between devices, shards(): lax.all_to_all(jnp.stack([feature_taps] * lax.axis_size(('ctx', 'fsdp')))...  22.1 us
    ppermute x8, starting transfers between devices, passed_along(): return lax.ppermute(shard, axis, pairs)  20.5 us
  transfers between devices with their start and end apart: 10, of which 1 were waited for; matrix products, arithmetic and copies ran while one was open for 10% of the time, Pallas kernels for 0%

profile of v1, /device:TPU:1, one launch (start us, length us, event | category | flops | bytes accessed | tf_op | source)
XLA Modules:
  0.0 712.0 jit_solution(2965443858461542242)
XLA Ops:
  8.7 4.6 collective-permute-start
  14.9 1.9 collective-permute-start.2
  16.8 2.8 stack.34
  19.6 22.1 %all-to-all-start = ((f32[512,3,3,4]{3,2,1,0:T(4,128)}), f32[512,3,3,4]{3,2,1,0:T(4,128)}, u32[]{:S(2)}, u32[]{:S(2)}) async-start(f32[512,3,3,4]{3,2,1,0:T(4,128)} %stack.34), calls=%async_computation | async-start | bytes 6291456 | tf_op jit(solution)/shard_map/all_to_all | solution.py:75
  42.4 3.5 collective-permute-start.1
  46.0 90.5 %all-gather = bf16[64,2,16]{2,1,0:T(2,128)(2,1)S(1)} all-gather(bf16[1,2,16]{2,1,0:T(2,128)(2,1)S(1)} %bitcast_convert_fusion), channel_id=1, replica_groups=mesh['ctx'=64,'fsdp'=8] {'ctx'}, dimensions={0}, use_global_device_ids=true | all-gather | bytes 4160 | tf_op jit(solution)/shard_map/all_gather | solution.py:72
  137.0 1.9 copy.35
  138.8 1.9 slice.244
  140.7 9.4 %reshape.125 = bf16[16,256,383]{2,1,0:T(8,128)(2,1)S(1)} reshape(bf16[16,98048]{1,0:T(8,128)(2,1)} %slice.244) | data formatting | bytes 6275072 | tf_op jit(solution)/shard_map/reshape | solution.py:50
  152.3 1.7 fusion.35
  154.0 1.7 fusion.36
  155.8 1.7 fusion.37
  157.5 3.5 copy.24
  161.0 3.6 reshape.122
  164.8 3.7 fusion.10
  169.2 1.9 collective-permute-start.3
  173.5 100.7 %all-reduce.6 = (f32[2048]{0:T(1024)}, f32[2048]{0:T(1024)}) all-reduce(f32[2048]{0:T(1024)S(1)} %dynamic-update-slice, f32[2048]{0:T(1024)S(1)} %multiply_dynamic-update-slice_fusion), channel_id=1, replica_groups=mesh['ctx'=64,'fsdp'=8] {'ctx','fsdp'}, use_global_device_ids=true, to_apply=%add.2 | all-reduce | flops 4096 | bytes 32768
  275.0 2.8 collective-permute-start.5
  281.0 2.5 fusion.12
  284.8 1.9 collective-permute-start.4
  289.2 2.5 fusion.41
  291.7 1.9 rev.14
  293.7 2.6 fusion.18
  296.9 1.9 collective-permute-start.6
  299.5 1.9 collective-permute-start.7
  302.4 15.6 %while.12 = (s32[]{:T(128)}, f32[4,4,128]{2,1,0:T(4,128)}, bf16[4,4,16,1,256]{4,2,1,3,0:T(8,128)(2,1)S(1)}, bf16[4,4,16,1,383]{4,2,1,3,0:T(8,128)(2,1)S(1)}, s32[]{:T(128)}, /*index=5*/f32[]{:T(128)}) while((s32[]{:T(128)}, f32[4,4,128]{2,1,0:T(4,128)}, bf16[4,4,16,1,256]{4,2,1,3,0:T(8,128)(2,1)S(1)}, ...), condition=%wide.region_2.3_spmd, body=%wide.region_0.2_spmd.sunk | while | flops 12680706 | bytes 13180045 | solution.py:150
  303.5 1.6 reshape.141
  307.4 1.6 reshape.141
  311.3 1.6 reshape.141
  318.8 125.7 %all-reduce.3 = f32[16,128]{1,0:T(8,128)S(1)} all-reduce(f32[16,128]{1,0:T(8,128)S(1)} %bitcast.110), channel_id=2, replica_groups=mesh['ctx'=64,'fsdp'=8] {'ctx'}, use_global_device_ids=true, to_apply=%region_3.4.clone | all-reduce | flops 2048 | bytes 16384
  447.6 1.7 fusion.27
  453.1 250.6 %all-reduce.9.cloned.1.call-done = f32[3,3,2048]{2,1,0:T(4,128)} async-done(((f32[3,3,2048]{2,1,0:T(4,128)}), f32[3,3,2048]{2,1,0:T(4,128)}) %all-reduce.9.cloned.1.call-update) | async-done | bytes 73744
  (151 shorter events, 38.5 us)
Async XLA Ops:
  8.7 147.0 %collective-permute-start = (bf16[256,2]{1,0:T(8,128)(2,1)}, bf16[256,2]{1,0:T(8,128)(2,1)}, u32[]{:S(2)}, u32[]{:S(2)}) collective-permute-start(bf16[256,2]{1,0:T(8,128)(2,1)} %slice.185), channel_id=1, source_target_pairs={{0,8},{8,16},{16,24},{24,32},{32,40},{40,48},{48,56},{56,64},{64,7... | collective-permute-start | bytes 3080 | tf_op jit(solution)/shard_map/ppermute | solution.py:11
  14.9 137.4 %collective-permute-start.2 = (bf16[256,2]{1,0:T(8,128)(2,1)}, bf16[256,2]{1,0:T(8,128)(2,1)}, u32[]{:S(2)}, u32[]{:S(2)}) collective-permute-start(bf16[256,2]{1,0:T(8,128)(2,1)} %slice.199), channel_id=1, source_target_pairs={{0,8},{8,16},{16,24},{24,32},{32,40},{40,48},{48,56},{56,64},{64,7... | collective-permute-start | bytes 3080 | tf_op jit(solution)/shard_map/ppermute | solution.py:11
  19.6 22.1 %copy-start.7 = (bf16[256,256]{1,0:T(8,128)(2,1)S(1)}, bf16[256,256]{1,0:T(8,128)(2,1)}, u32[]{:S(2)}) copy-start(bf16[256,256]{1,0:T(8,128)(2,1)} %param.10) | copy-start | bytes 393220
  19.6 26.4 %copy-start.28 = (f32[16,2]{0,1:T(2,128)S(1)}, f32[16,2]{0,1:T(2,128)}, u32[]{:S(2)}) copy-start(f32[16,2]{0,1:T(2,128)} %param.13) | copy-start | bytes 388
  19.6 137.9 %all-to-all-start = ((f32[512,3,3,4]{3,2,1,0:T(4,128)}), f32[512,3,3,4]{3,2,1,0:T(4,128)}, u32[]{:S(2)}, u32[]{:S(2)}) async-start(f32[512,3,3,4]{3,2,1,0:T(4,128)} %stack.34), calls=%async_computation | async-start | bytes 6291456 | tf_op jit(solution)/shard_map/all_to_all | solution.py:75
  41.7 662.1 %all-reduce.9.cloned.1.call-start = ((), (), s32[]{:S(2)}) async-start(), calls=%async_computation.1 | async-start | bytes 196608
  42.4 111.6 %collective-permute-start.1 = (bf16[256,2]{1,0:T(8,128)(2,1)}, bf16[256,2]{1,0:T(8,128)(2,1)}, u32[]{:S(2)}, u32[]{:S(2)}) collective-permute-start(bf16[256,2]{1,0:T(8,128)(2,1)} %slice.192), channel_id=1, source_target_pairs={{0,8},{8,16},{16,24},{24,32},{32,40},{40,48},{48,56},{56,64},{64,7... | collective-permute-start | bytes 3080 | tf_op jit(solution)/shard_map/ppermute | solution.py:11
  140.7 11.3 %copy-start.29 = (f32[4]{0:T(128)S(1)}, f32[4]{0:T(128)}, u32[]{:S(2)}) copy-start(f32[4]{0:T(128)} %param.15) | copy-start | bytes 52
  140.7 11.6 %copy-start.6 = (bf16[256,256]{1,0:T(8,128)(2,1)S(1)}, bf16[256,256]{1,0:T(8,128)(2,1)}, u32[]{:S(2)}) copy-start(bf16[256,256]{1,0:T(8,128)(2,1)} %param.11) | copy-start | bytes 393220
  140.7 15.1 %copy-start.3 = (bf16[256,256]{1,0:T(8,128)(2,1)S(1)}, bf16[256,256]{1,0:T(8,128)(2,1)}, u32[]{:S(2)}) copy-start(bf16[256,256]{1,0:T(8,128)(2,1)} %param.9) | copy-start | bytes 393220
  164.7 6.6 copy-start.12
  164.7 6.6 copy-start.14
  164.7 6.6 copy-start.16
  164.7 6.6 copy-start.18
  164.7 6.6 copy-start.20
  164.8 6.6 copy-start.22
  164.8 6.6 copy-start.24
  169.2 109.9 %collective-permute-start.3 = (bf16[256,127]{1,0:T(8,128)(2,1)}, bf16[256,127]{1,0:T(8,128)(2,1)}, u32[]{:S(2)}, u32[]{:S(2)}) collective-permute-start(bf16[256,127]{1,0:T(8,128)(2,1)} %slice.242), channel_id=1, source_target_pairs={{0,8},{8,16},{16,24},{24,32},{32,40},{40,48},{48,56},{56,64},{64,7... | collective-permute-start | bytes 195080 | tf_op jit(solution)/shard_map/ppermute | solution.py:11
  274.2 6.7 copy-start
  274.2 6.7 copy-start.10
  275.0 11.7 %collective-permute-start.5 = (bf16[256,127]{1,0:T(8,128)(2,1)}, bf16[256,127]{1,0:T(8,128)(2,1)S(1)}, u32[]{:S(2)}, u32[]{:S(2)}) collective-permute-start(bf16[256,127]{1,0:T(8,128)(2,1)} %slice.249), channel_id=1, source_target_pairs={{8,0},{16,8},{24,16},{32,24},{40,32},{48,40},{56,48},{64,56},{72,6... | collective-permute-start | bytes 195080 | tf_op jit(solution)/shard_map/ppermute | solution.py:11
  284.8 161.9 %collective-permute-start.4 = (bf16[256,2]{1,0:T(8,128)(2,1)}, bf16[256,2]{1,0:T(8,128)(2,1)}, u32[]{:S(2)}, u32[]{:S(2)}) collective-permute-start(bf16[256,2]{1,0:T(8,128)(2,1)} %slice.245), channel_id=1, source_target_pairs={{8,0},{16,8},{24,16},{32,24},{40,32},{48,40},{56,48},{64,56},{72,6... | collective-permute-start | bytes 3080 | tf_op jit(solution)/shard_map/ppermute | solution.py:11
  296.9 152.3 %collective-permute-start.6 = (bf16[256,2]{1,0:T(8,128)(2,1)}, bf16[256,2]{1,0:T(8,128)(2,1)}, u32[]{:S(2)}, u32[]{:S(2)}) collective-permute-start(bf16[256,2]{1,0:T(8,128)(2,1)} %slice.251), channel_id=1, source_target_pairs={{8,0},{16,8},{24,16},{32,24},{40,32},{48,40},{56,48},{64,56},{72,6... | collective-permute-start | bytes 3080 | tf_op jit(solution)/shard_map/ppermute | solution.py:11
  299.5 151.8 %collective-permute-start.7 = (bf16[256,2]{1,0:T(8,128)(2,1)}, bf16[256,2]{1,0:T(8,128)(2,1)}, u32[]{:S(2)}, u32[]{:S(2)}) collective-permute-start(bf16[256,2]{1,0:T(8,128)(2,1)} %slice.255), channel_id=1, source_target_pairs={{8,0},{16,8},{24,16},{32,24},{40,32},{48,40},{56,48},{64,56},{72,6... | collective-permute-start | bytes 3080 | tf_op jit(solution)/shard_map/ppermute | solution.py:11
  302.4 144.4 %copy-start.5 = (bf16[256,256]{1,0:T(8,128)(2,1)S(1)}, bf16[256,256]{1,0:T(8,128)(2,1)}, u32[]{:S(2)}) copy-start(bf16[256,256]{1,0:T(8,128)(2,1)} %copy-done.4) | copy-start | bytes 393220
  302.4 145.3 %copy-start.25 = (f32[1,1,256]{2,1,0:T(1,128)S(1)}, f32[1,1,256]{2,1,0:T(1,128)}, u32[]{:S(2)}) copy-start(f32[1,1,256]{2,1,0:T(1,128)} %copy-done.24) | copy-start | bytes 3076
  302.4 147.9 %copy-start.19 = (f32[1,1,256]{2,1,0:T(1,128)S(1)}, f32[1,1,256]{2,1,0:T(1,128)}, u32[]{:S(2)}) copy-start(f32[1,1,256]{2,1,0:T(1,128)} %copy-done.18) | copy-start | bytes 3076
  302.4 147.9 %copy-start.21 = (f32[1,1,256]{2,1,0:T(1,128)S(1)}, f32[1,1,256]{2,1,0:T(1,128)}, u32[]{:S(2)}) copy-start(f32[1,1,256]{2,1,0:T(1,128)} %copy-done.20) | copy-start | bytes 3076
  302.4 147.9 %copy-start.23 = (f32[1,1,256]{2,1,0:T(1,128)S(1)}, f32[1,1,256]{2,1,0:T(1,128)}, u32[]{:S(2)}) copy-start(f32[1,1,256]{2,1,0:T(1,128)} %copy-done.22) | copy-start | bytes 3076
  318.0 134.1 %copy-start.13 = (f32[1,1,256]{2,1,0:T(1,128)S(1)}, f32[1,1,256]{2,1,0:T(1,128)}, u32[]{:S(2)}) copy-start(f32[1,1,256]{2,1,0:T(1,128)} %copy-done.12) | copy-start | bytes 3076
  318.0 134.1 %copy-start.15 = (f32[1,1,256]{2,1,0:T(1,128)S(1)}, f32[1,1,256]{2,1,0:T(1,128)}, u32[]{:S(2)}) copy-start(f32[1,1,256]{2,1,0:T(1,128)} %copy-done.14) | copy-start | bytes 3076
  318.0 134.1 %copy-start.17 = (f32[1,1,256]{2,1,0:T(1,128)S(1)}, f32[1,1,256]{2,1,0:T(1,128)}, u32[]{:S(2)}) copy-start(f32[1,1,256]{2,1,0:T(1,128)} %copy-done.16) | copy-start | bytes 3076
  (14 other events, 31.8 us)
Sparse Core Ops, SparseCore 0:
  446.8 256.8 all-reduce.8
